TPU v7x, 256 devices: a whole 4x4x8 slice. The times are simulated.
256 devices in a mesh: row: 8 (over x, core), col: 32 (over y, z).
Axes of the slice: x: 4, y: 4, z: 8, core: 2. Of those that a mesh axis runs over, the one named last changes fastest.
Arguments:
- tokens: bfloat16 [1024, 6144], P('col', 'row'), may hold values from -6 to 6
- w_up: bfloat16 [6144, 24576], P('row', 'col'), may hold values from -0.078125 to 0.078125
- w_down: bfloat16 [24576, 6144], P('col', 'row'), may hold values from -0.0390625 to 0.0390625
- expert_in: bfloat16 [6144, 8192], P(None, 'col'), may hold values from -0.078125 to 0.078125
- expert_out: bfloat16 [8192, 6144], P('col'), may hold values from -0.125 to 0.125
- expert_ids: int32 [1024, 2], P('col'), may hold values from 0 to 3, as said below
- route_weights: bfloat16 [1024, 2], P('col'), may hold values from 0.25 to 1
- out_grad: bfloat16 [1024, 6144], P('col', 'row'), may hold values from -6 to 6
Outputs:
- layer_out: bfloat16 [1024, 6144], P('col', 'row')
- tokens_grad: bfloat16 [1024, 6144], P('col', 'row')
- up_grad: bfloat16 [6144, 24576], P('row', 'col')
- down_grad: bfloat16 [24576, 6144], P('col', 'row')
- expert_in_grad: bfloat16 [6144, 8192], P('row', 'col')
- expert_out_grad: bfloat16 [8192, 6144], P('col', 'row')
Inputs may be any that keep to these rules, and one draw needn't show every extreme that they name: `expert_ids`: the two experts of a token differ. In every aligned block of 4 tokens no expert is named by more than 3 of the block's pairs; one expert is named by exactly 3 pairs, the same expert in all blocks whose index leaves the same remainder modulo 32 // 4; the other experts' counts in a block differ by at most one. Every expert is named somewhere.
All inputs are finite; a program needn't handle non-finite values.
Results may differ from a plain program's by a relative error of at most 0.025.
Values may be sent and summed in bfloat16 or wider, within the bound.
No kernel may reach another device: no remote copies, remote signals or barrier semaphores. Data moves between devices by JAX's collectives and lax.ppermute only.
A program may use at most 128 MiB of HBM per device.

v0:
```python
import jax
import jax.numpy as jnp
from jax import lax
from jax.sharding import PartitionSpec as P

EXPERTS = 4
gelu_scale = 0.7978845608028654
gelu_cubic = 0.044715


def gelu_tanh(value):
    return 0.5 * value * (1.0 + jnp.tanh(gelu_scale * (value + gelu_cubic * value * value * value)))


def gelu_slope(value):
    inner = jnp.tanh(gelu_scale * (value + gelu_cubic * value * value * value))
    return 0.5 * (1.0 + inner) + 0.5 * value * (1.0 - inner * inner) * gelu_scale * (
        1.0 + 3.0 * gelu_cubic * value * value
    )


def slot_ranks(pairs):
    count = pairs.shape[-1]
    positions = jnp.arange(count, dtype=jnp.int32)
    earlier = positions[:, None] > positions[None, :]
    matching = pairs[..., :, None] == pairs[..., None, :]
    return jnp.sum((matching & earlier).astype(jnp.int32), axis=-1)


def gather_rows(part, axis_name):
    count = lax.axis_size(axis_name)
    spread = jnp.broadcast_to(part[None], (count,) + part.shape)
    got = lax.all_to_all(spread, axis_name, 0, 0, tiled=True)
    return got.reshape((count * part.shape[0],) + part.shape[1:])


def scatter_sum(terms, axis_name):
    count = lax.axis_size(axis_name)
    blocks = terms.astype(jnp.bfloat16).reshape((count, terms.shape[0] // count) + terms.shape[1:])
    got = lax.all_to_all(blocks, axis_name, 0, 0, tiled=True)
    return got.astype(jnp.float32).sum(axis=0)


def scatter_sum_cols(terms, axis_name):
    count = lax.axis_size(axis_name)
    got = lax.all_to_all(terms.astype(jnp.bfloat16), axis_name, 1, 0, tiled=True)
    return (
        got.reshape((count, terms.shape[0], terms.shape[1] // count))
        .astype(jnp.float32)
        .sum(axis=0)
    )


def dense_exchange(payload, axis_name):
    shape = payload.shape
    flat = payload.reshape(shape[0], -1, 128)
    got = lax.all_to_all(flat, axis_name, 0, 0, tiled=True)
    return got.reshape(shape)


def swap_blocks(pair, count):
    arrays, tok, width = pair.shape
    block = tok // count
    parts = pair.reshape(arrays, count, block, width).transpose(1, 0, 2, 3)
    got = lax.all_to_all(parts.reshape(count, arrays * block, width), "row", 0, 0, tiled=True)
    got = got.reshape(count, arrays, block, width).transpose(1, 2, 0, 3)
    return got.reshape(arrays, block, count * width)


def unswap_blocks(pair, count):
    arrays, block, full = pair.shape
    width = full // count
    parts = pair.reshape(arrays, block, count, width).transpose(2, 0, 1, 3)
    got = lax.all_to_all(parts.reshape(count, arrays * block, width), "row", 0, 0, tiled=True)
    got = got.reshape(count, arrays, block, width).transpose(1, 0, 2, 3)
    return got.reshape(arrays, count * block, width)


def on_device(tokens, w_up, w_down, expert_in, expert_out, expert_ids, route_weights, out_grad):
    row_count = lax.axis_size("row")
    col_count = lax.axis_size("col")
    tok_col = tokens.shape[0]
    block_len = tok_col // row_count
    group_len = col_count // EXPERTS
    slot_cap = max(2, 3 * block_len // 4)
    model_width = expert_out.shape[1]
    my_row = lax.axis_index("row")
    own_grad = swap_blocks(out_grad[None], row_count)[0]
    ids_own = lax.dynamic_slice_in_dim(expert_ids, my_row * block_len, block_len, 0)
    weights_own = lax.dynamic_slice_in_dim(route_weights, my_row * block_len, block_len, 0)
    expert_range = jnp.arange(EXPERTS, dtype=jnp.int32)
    weight_table = jnp.sum(
        weights_own.astype(jnp.float32)[None, :, :]
        * (ids_own[None, :, :] == expert_range[:, None, None]).astype(jnp.float32),
        axis=2,
    )
    table_row = jnp.pad(
        weight_table.reshape(1, EXPERTS * block_len).astype(jnp.bfloat16),
        ((0, 0), (0, model_width - EXPERTS * block_len)),
    )
    grad_pack = jnp.concatenate([own_grad, table_row], axis=0)
    tokens_ready, grad_pack = lax.optimization_barrier((tokens, grad_pack))
    tok_panel = gather_rows(tokens_ready, "col")
    pack_all = lax.all_gather(grad_pack, "col", axis=0, tiled=False)
    my_expert = lax.axis_index("col") // group_len
    weights_recv = lax.dynamic_slice_in_dim(
        pack_all[:, block_len, : EXPERTS * block_len], my_expert * block_len, block_len, 1
    )
    grad_rows_in = (
        weights_recv.astype(jnp.float32)[:, :, None] * pack_all[:, :block_len].astype(jnp.float32)
    ).astype(jnp.bfloat16)
    up_terms = jnp.dot(tok_panel, w_up, preferred_element_type=jnp.float32)
    preact = scatter_sum(up_terms, "row")
    hidden_full = gather_rows(gelu_tanh(preact).astype(jnp.bfloat16), "row")
    rows_in = hidden_full
    down_terms, pack_all = lax.optimization_barrier(
        (jnp.dot(rows_in, w_down, preferred_element_type=jnp.float32), pack_all)
    )
    dense_term = scatter_sum(down_terms, "col")
    mixed_act = (tokens.astype(jnp.float32) + dense_term).astype(jnp.bfloat16)
    own_rows = swap_blocks(mixed_act[None], row_count)[0]
    scaled_flat = grad_rows_in.reshape(col_count * block_len, model_width)
    payload = jnp.broadcast_to(own_rows[None], (col_count,) + own_rows.shape)
    got = lax.all_to_all(payload, "col", 0, 0, tiled=True)
    got_flat = got.reshape(col_count * block_len, model_width)
    hid_units = expert_in.shape[1]
    e_pre = jnp.dot(got_flat, expert_in, preferred_element_type=jnp.float32).reshape(
        col_count, block_len, hid_units
    )
    g_dot = jnp.dot(scaled_flat, expert_out.T, preferred_element_type=jnp.float32).reshape(
        col_count, block_len, hid_units
    )
    e_hidden = gelu_tanh(e_pre).astype(jnp.bfloat16)
    e_dpre = (g_dot * gelu_slope(e_pre)).astype(jnp.bfloat16)
    blank = jnp.zeros_like(e_hidden)

    def at_rows(value, first):
        halves = [value, blank] if first else [blank, value]
        return jnp.concatenate(halves, axis=1).reshape(col_count * 2 * block_len, hid_units)

    back_flat = jnp.dot(
        at_rows(e_hidden, True), expert_out, preferred_element_type=jnp.float32
    ) + jnp.dot(at_rows(e_dpre, False), expert_in.T, preferred_element_type=jnp.float32)
    grad_in = jnp.dot(
        got_flat.T,
        e_dpre.reshape(col_count * block_len, hid_units),
        preferred_element_type=jnp.float32,
    )
    grad_out = jnp.dot(
        e_hidden.reshape(col_count * block_len, hid_units).T,
        scaled_flat,
        preferred_element_type=jnp.float32,
    )
    back = (
        lax.all_to_all(
            back_flat.astype(jnp.bfloat16)
            .reshape(col_count, 2 * block_len, row_count, model_width // row_count)
            .transpose(2, 0, 1, 3)
            .reshape(row_count * col_count, 2 * block_len, model_width // row_count),
            ("row", "col"),
            0,
            0,
            tiled=True,
        )
        .astype(jnp.float32)
        .reshape(row_count, col_count, 2 * block_len, model_width // row_count)
    )
    local_table = jnp.sum(
        route_weights.astype(jnp.float32)[:, None, :]
        * (expert_ids[:, None, :] == expert_range[None, :, None]).astype(jnp.float32),
        axis=2,
    )
    source_weights = jnp.repeat(
        local_table.reshape(row_count, block_len, EXPERTS).transpose(0, 2, 1), group_len, axis=1
    )
    moe_sum = jnp.sum(source_weights[:, :, :, None] * back[:, :, :block_len], axis=1)
    grad_sum = jnp.sum(back[:, :, block_len:], axis=1)
    layer_out = (mixed_act.astype(jnp.float32) + moe_sum.reshape(tok_col, -1)).astype(jnp.bfloat16)
    mixed_grad = (out_grad.astype(jnp.float32) + grad_sum.reshape(tok_col, -1)).astype(jnp.bfloat16)
    expert_in_grad = lax.psum_scatter(
        grad_in.astype(jnp.bfloat16).astype(jnp.float32), "row", scatter_dimension=0, tiled=True
    ).astype(jnp.bfloat16)
    expert_out_grad = lax.psum_scatter(
        grad_out.astype(jnp.bfloat16).astype(jnp.float32), "row", scatter_dimension=1, tiled=True
    ).astype(jnp.bfloat16)
    cot_panel = gather_rows(mixed_grad, "col")
    hgrad_terms = jnp.dot(cot_panel, w_down.T, preferred_element_type=jnp.float32)
    down_grad = jnp.dot(hidden_full.T, cot_panel, preferred_element_type=jnp.float32).astype(
        jnp.bfloat16
    )
    hidden_grad = scatter_sum(hgrad_terms, "row")
    dpre_full = gather_rows((hidden_grad * gelu_slope(preact)).astype(jnp.bfloat16), "row")
    up_grad = jnp.dot(tok_panel.T, dpre_full, preferred_element_type=jnp.float32).astype(
        jnp.bfloat16
    )
    rows_in = dpre_full
    input_term = scatter_sum(jnp.dot(rows_in, w_up.T, preferred_element_type=jnp.float32), "col")
    tokens_grad = (mixed_grad.astype(jnp.float32) + input_term).astype(jnp.bfloat16)
    return (layer_out, tokens_grad, up_grad, down_grad, expert_in_grad, expert_out_grad)


def solution(mesh):
    in_specs = (
        P("col", "row"),
        P("row", "col"),
        P("col", "row"),
        P(None, "col"),
        P("col", None),
        P("col", None),
        P("col", None),
        P("col", "row"),
    )
    out_specs = (
        P("col", "row"),
        P("col", "row"),
        P("row", "col"),
        P("col", "row"),
        P("row", "col"),
        P("col", "row"),
    )
    return jax.shard_map(
        on_device, mesh=mesh, in_specs=in_specs, out_specs=out_specs, check_vma=False
    )
```

profile of v0, /device:TPU:32, one launch (start us, length us, event | category | flops | bytes accessed | tf_op | source)
XLA Modules:
  0.0 489.2 jit_solution(7330491538299597089)
XLA Ops:
  7.2 1.6 reshape_transpose_reshape_broadcast_in_dim.6
  8.8 4.3 all-to-all-start
  13.1 0.7 constant_dynamic-slice_fusion.2
  13.8 0.7 fusion.33
  14.7 4.0 all-to-all-done
  18.6 0.7 fusion.32
  19.3 2.1 broadcast_in_dim.14
  21.4 11.4 %all-to-all-start.1 = ((bf16[32,32,768]{2,1,0:T(8,128)(2,1)}), bf16[32,32,768]{2,1,0:T(8,128)(2,1)}, u32[]{:S(2)}, u32[]{:S(2)}) async-start(bf16[32,32,768]{2,1,0:T(8,128)(2,1)} %broadcast_in_dim.14), calls=%async_computation.1 | async-start | bytes 3145728 | tf_op jit(solution)/shard_map/all_to_all | solution.py:33
  32.9 0.7 all-gather.4.cloned.1.call-update
  33.6 41.8 %all-to-all-done.1 = bf16[32,32,768]{2,1,0:T(8,128)(2,1)} async-done(((bf16[32,32,768]{2,1,0:T(8,128)(2,1)}), bf16[32,32,768]{2,1,0:T(8,128)(2,1)}, u32[]{:S(2)}, u32[]{:S(2)}) %all-to-all-start.1) | async-done | bytes 1572896 | tf_op jit(solution)/shard_map/all_to_all | solution.py:33
  75.4 3.1 convolution_convert_fusion.2
  78.5 24.0 %all_to_all.60 = bf16[8,128,768]{2,1,0:T(8,128)(2,1)S(1)} all-to-all(bf16[8,128,768]{2,1,0:T(8,128)(2,1)S(1)} %bitcast.88), channel_id=1, replica_groups=mesh['row'=8,'col'=32] {'row'}, dimensions={0} | all-to-all | bytes 3145728 | tf_op jit(solution)/shard_map/all_to_all | solution.py:40
  103.0 24.2 %all_to_all.61 = bf16[8,128,768]{2,1,0:T(8,128)(2,1)S(1)} all-to-all(bf16[8,128,768]{2,1,0:T(8,128)(2,1)S(1)} %broadcast_in_dim.15), channel_id=1, replica_groups=mesh['row'=8,'col'=32] {'row'}, dimensions={0} | all-to-all | bytes 3145728 | tf_op jit(solution)/shard_map/all_to_all | solution.py:33
  127.2 1.2 copy-done.4
  128.4 2.5 fusion.36
  130.9 45.4 %all_to_all.62 = bf16[32,32,768]{2,1,0:T(8,128)(2,1)S(1)} all-to-all(bf16[32,32,768]{2,1,0:T(8,128)(2,1)} %bitcast.87), channel_id=1, replica_groups=mesh['row'=8,'col'=32] {'col'}, dimensions={0} | all-to-all | bytes 3145728 | tf_op jit(solution)/shard_map/all_to_all | solution.py:40
  177.8 1.4 reshape_transpose_reshape_broadcast_in_dim.7
  179.2 8.8 %all_to_all.63 = bf16[8,4,768]{2,1,0:T(4,128)(2,1)S(1)} all-to-all(bf16[8,4,768]{2,1,0:T(4,128)(2,1)} %reshape_transpose_reshape_broadcast_in_dim.7), channel_id=1, replica_groups=mesh['row'=8,'col'=32] {'row'}, dimensions={0} | all-to-all | bytes 98304 | tf_op jit(solution)/shard_map/all_to_all | solution.py:65
  188.0 1.9 broadcast_in_dim.18
  189.8 4.9 %all-to-all-start.6 = ((bf16[32,4,6144]{2,1,0:T(4,128)(2,1)}), bf16[32,4,6144]{2,1,0:T(4,128)(2,1)}, u32[]{:S(2)}, u32[]{:S(2)}) async-start(bf16[32,4,6144]{2,1,0:T(4,128)(2,1)} %broadcast_in_dim.18), calls=%async_computation.6 | async-start | bytes 3145728 | tf_op jit(solution)/shard_map/all_to_all | solution.py:124
  195.0 0.9 slice.16
  196.6 3.7 slice.17
  200.3 33.5 %all-to-all-done.6 = bf16[32,4,6144]{2,1,0:T(4,128)(2,1)} async-done(((bf16[32,4,6144]{2,1,0:T(4,128)(2,1)}), bf16[32,4,6144]{2,1,0:T(4,128)(2,1)}, u32[]{:S(2)}, u32[]{:S(2)}) %all-to-all-start.6) | async-done | bytes 1572896 | tf_op jit(solution)/shard_map/all_to_all | solution.py:124
  233.9 3.4 multiply_convert_fusion.8
  238.0 4.1 fusion.4
  242.1 0.9 copy.69
  243.0 4.0 fusion.15
  247.6 1.0 fusion.31
  248.6 1.1 fusion
  249.7 1.8 copy.64
  251.5 7.0 %all-to-all-start.7 = ((bf16[256,8,768]{2,1,0:T(8,128)(2,1)}), bf16[256,8,768]{2,1,0:T(8,128)(2,1)S(1)}, u32[]{:S(2)}, u32[]{:S(2)}) async-start(bf16[256,8,768]{2,1,0:T(8,128)(2,1)} %bitcast.20), calls=%async_computation.7 | async-start | bytes 6291456 | tf_op jit(solution)/shard_map/all_to_all | solution.py:155
  258.6 5.5 %fusion.2 = f32[6144,256]{1,0:T(8,128)} fusion(bf16[32,4,256]{2,0,1:T(8,128)(2,1)} %copy-done.16, bf16[32,4,6144]{2,1,0:T(4,128)(2,1)} %all-to-all-done.6), kind=kOutput, calls=%fused_computation.5 | convolution fusion | flops 405798912 | bytes 7929856 | tf_op jit(solution)/shard_map/dot_general | solution.py:144
  265.4 0.8 reshape.142
  266.1 0.7 broadcast_bitcast_fusion
  266.8 67.2 %all-to-all-done.7 = bf16[256,8,768]{2,1,0:T(8,128)(2,1)S(1)} async-done(((bf16[256,8,768]{2,1,0:T(8,128)(2,1)}), bf16[256,8,768]{2,1,0:T(8,128)(2,1)S(1)}, u32[]{:S(2)}, u32[]{:S(2)}) %all-to-all-start.7) | async-done | bytes 3145760 | tf_op jit(solution)/shard_map/all_to_all | solution.py:155
  334.9 2.3 slice_reduce_fusion
  338.0 45.0 %all_to_all.64 = bf16[32,32,768]{2,1,0:T(8,128)(2,1)S(1)} all-to-all(bf16[32,32,768]{2,1,0:T(8,128)(2,1)S(1)} %broadcast_in_dim.19), channel_id=1, replica_groups=mesh['row'=8,'col'=32] {'col'}, dimensions={0} | all-to-all | bytes 3145728 | tf_op jit(solution)/shard_map/all_to_all | solution.py:33
  383.0 1.4 convolution_convert_fusion.1
  384.4 24.4 %all_to_all.65 = bf16[8,128,768]{2,1,0:T(8,128)(2,1)S(1)} all-to-all(bf16[8,128,768]{2,1,0:T(8,128)(2,1)S(1)} %bitcast.89), channel_id=1, replica_groups=mesh['row'=8,'col'=32] {'row'}, dimensions={0} | all-to-all | bytes 3145728 | tf_op jit(solution)/shard_map/all_to_all | solution.py:40
  409.4 24.2 %all_to_all.66 = bf16[8,128,768]{2,1,0:T(8,128)(2,1)S(1)} all-to-all(bf16[8,128,768]{2,1,0:T(8,128)(2,1)S(1)} %broadcast_in_dim.20), channel_id=1, replica_groups=mesh['row'=8,'col'=32] {'row'}, dimensions={0} | all-to-all | bytes 3145728 | tf_op jit(solution)/shard_map/all_to_all | solution.py:33
  433.6 2.6 convolution_convert_fusion
  436.2 5.1 %all-to-all-start.11 = ((bf16[32,32,768]{2,1,0:T(8,128)(2,1)}), bf16[32,32,768]{2,1,0:T(8,128)(2,1)}, u32[]{:S(2)}, u32[]{:S(2)}) async-start(bf16[32,32,768]{2,1,0:T(8,128)(2,1)} %bitcast.26), calls=%async_computation.11 | async-start | bytes 3145728 | tf_op jit(solution)/shard_map/all_to_all | solution.py:40
  442.0 2.5 convolution_convert_fusion.3
  444.5 3.9 convolution_convert_fusion.4
  448.3 2.1 convert_element_type.172
  450.4 1.9 convert_element_type.169
  452.3 28.1 %all-to-all-done.11 = bf16[32,32,768]{2,1,0:T(8,128)(2,1)} async-done(((bf16[32,32,768]{2,1,0:T(8,128)(2,1)}), bf16[32,32,768]{2,1,0:T(8,128)(2,1)}, u32[]{:S(2)}, u32[]{:S(2)}) %all-to-all-start.11) | async-done | bytes 1572896 | tf_op jit(solution)/shard_map/all_to_all | solution.py:40
  480.4 1.6 convert_reduce_fusion
  (77 shorter events, 9.2 us)
Async XLA Ops:
  7.2 226.7 %copy-start = (bf16[6144,256]{1,0:T(8,128)(2,1)S(1)}, bf16[6144,256]{1,0:T(8,128)(2,1)}, u32[]{:S(2)}) copy-start(bf16[6144,256]{1,0:T(8,128)(2,1)} %param.11) | copy-start | bytes 9437188
  8.8 9.8 %all-to-all-start = ((bf16[8,4,768]{2,1,0:T(4,128)(2,1)}), bf16[8,4,768]{2,1,0:T(4,128)(2,1)S(1)}, u32[]{:S(2)}, u32[]{:S(2)}) async-start(bf16[8,4,768]{2,1,0:T(4,128)(2,1)} %reshape_transpose_reshape_broadcast_in_dim.6), calls=%async_computation | async-start | bytes 98304 | tf_op jit(solution)/shard_map/all_to_all | solution.py:65
  21.4 54.0 %all-to-all-start.1 = ((bf16[32,32,768]{2,1,0:T(8,128)(2,1)}), bf16[32,32,768]{2,1,0:T(8,128)(2,1)}, u32[]{:S(2)}, u32[]{:S(2)}) async-start(bf16[32,32,768]{2,1,0:T(8,128)(2,1)} %broadcast_in_dim.14), calls=%async_computation.1 | async-start | bytes 3145728 | tf_op jit(solution)/shard_map/all_to_all | solution.py:33
  32.8 98.1 %all-gather.4.cloned.1.call-start = ((), (), s32[]{:S(2)}) async-start(), calls=%async_computation.16 | async-start | bytes 3244032 | tf_op jit(solution)/shard_map/all_gather | solution.py:104
  103.0 25.4 %copy-start.20 = (bf16[768,768]{1,0:T(8,128)(2,1)S(1)}, bf16[768,768]{1,0:T(8,128)(2,1)}, u32[]{:S(2)}) copy-start(bf16[768,768]{1,0:T(8,128)(2,1)} %param.10) | copy-start | bytes 3538948
  127.2 1.2 copy-start.4
  176.3 0.8 copy-start.14
  189.8 44.0 %all-to-all-start.6 = ((bf16[32,4,6144]{2,1,0:T(4,128)(2,1)}), bf16[32,4,6144]{2,1,0:T(4,128)(2,1)}, u32[]{:S(2)}, u32[]{:S(2)}) async-start(bf16[32,4,6144]{2,1,0:T(4,128)(2,1)} %broadcast_in_dim.18), calls=%async_computation.6 | async-start | bytes 3145728 | tf_op jit(solution)/shard_map/all_to_all | solution.py:124
  194.7 253.6 %reduce-scatter.5.cloned.1.call-start = ((), (), s32[]{:S(2)}) async-start(), calls=%async_computation.15 | async-start | bytes 7077888 | tf_op jit(solution)/shard_map/reduce_scatter | solution.py:183
  196.6 3.7 copy-start.17
  233.9 4.1 copy-start.2
  237.3 0.6 copy-start.13
  243.0 4.6 copy-start.3
  247.0 0.6 copy-start.16
  251.5 82.4 %all-to-all-start.7 = ((bf16[256,8,768]{2,1,0:T(8,128)(2,1)}), bf16[256,8,768]{2,1,0:T(8,128)(2,1)S(1)}, u32[]{:S(2)}, u32[]{:S(2)}) async-start(bf16[256,8,768]{2,1,0:T(8,128)(2,1)} %bitcast.20), calls=%async_computation.7 | async-start | bytes 6291456 | tf_op jit(solution)/shard_map/all_to_all | solution.py:155
  258.6 191.8 %reduce-scatter.3.cloned.1.call-start = ((), (), s32[]{:S(2)}) async-start(), calls=%async_computation.14 | async-start | bytes 7077888 | tf_op jit(solution)/shard_map/reduce_scatter | solution.py:180
  264.1 0.7 copy-start.19
  264.1 0.7 copy-start.18
  334.0 0.9 copy-start.8
  334.9 2.3 copy-start.15
  337.2 0.6 copy-start.9
  338.0 45.0 %copy-start.21 = (bf16[768,768]{1,0:T(8,128)(2,1)S(1)}, bf16[768,768]{1,0:T(8,128)(2,1)}, u32[]{:S(2)}) copy-start(bf16[768,768]{1,0:T(8,128)(2,1)} %param.10) | copy-start | bytes 3538948
  409.4 24.2 %copy-start.22 = (bf16[768,768]{1,0:T(8,128)(2,1)S(1)}, bf16[768,768]{1,0:T(8,128)(2,1)}, u32[]{:S(2)}) copy-start(bf16[768,768]{1,0:T(8,128)(2,1)} %param.9) | copy-start | bytes 3538948
  433.6 2.6 copy-start.6
  436.2 5.1 %copy-start.12 = (f32[8,4,768]{2,1,0:T(4,128)S(1)}, f32[8,4,768]{2,1,0:T(4,128)}, u32[]{:S(2)}) copy-start(f32[8,4,768]{2,1,0:T(4,128)} %get-tuple-element.13) | copy-start | bytes 294916
  436.2 5.2 %copy-start.11 = (bf16[32,768]{1,0:T(8,128)(2,1)S(1)}, bf16[32,768]{1,0:T(8,128)(2,1)}, u32[]{:S(2)}) copy-start(bf16[32,768]{1,0:T(8,128)(2,1)} %add_convert_fusion.3) | copy-start | bytes 147460
  436.2 5.8 %copy-start.5 = (bf16[8,128,768]{2,1,0:T(8,128)(2,1)S(1)}, bf16[8,128,768]{2,1,0:T(8,128)(2,1)}, u32[]{:S(2)}) copy-start(bf16[8,128,768]{2,1,0:T(8,128)(2,1)} %copy-done.4) | copy-start | bytes 4718596
  436.2 44.2 %all-to-all-start.11 = ((bf16[32,32,768]{2,1,0:T(8,128)(2,1)}), bf16[32,32,768]{2,1,0:T(8,128)(2,1)}, u32[]{:S(2)}, u32[]{:S(2)}) async-start(bf16[32,32,768]{2,1,0:T(8,128)(2,1)} %bitcast.26), calls=%async_computation.11 | async-start | bytes 3145728 | tf_op jit(solution)/shard_map/all_to_all | solution.py:40
  442.0 2.5 copy-start.7
  448.3 34.4 %copy-start.1 = (bf16[6144,256]{1,0:T(8,128)(2,1)S(1)}, bf16[6144,256]{1,0:T(8,128)(2,1)}, u32[]{:S(2)}) copy-start(bf16[6144,256]{1,0:T(8,128)(2,1)} %param.11) | copy-start | bytes 9437188
  450.4 31.7 %copy-start.10 = (bf16[32,768]{1,0:T(8,128)(2,1)S(1)}, bf16[32,768]{1,0:T(8,128)(2,1)}, u32[]{:S(2)}) copy-start(bf16[32,768]{1,0:T(8,128)(2,1)} %copy-done.9) | copy-start | bytes 147460
Sparse Core Ops, SparseCore 0:
  36.8 79.9 all-gather.3
  242.2 62.4 reduce-scatter.4
  307.3 50.1 reduce-scatter.2
where the time goes:
time: 491 us; the launch traced here: 489 us
  blocking collectives  196 us (40%)
  waiting for transfers between devices  175 us (36%)
  matrix products  35.1 us (7%)
  starting transfers between devices  33 us (7%)
  local copies, waits for them, and re-layouts  22.5 us (5%)
  between operations  14 us (3%)
  other arithmetic  13.4 us (3%)
    all_to_all x3, blocking collectives, scatter_sum(): got = lax.all_to_all(blocks, axis_name, 0, 0, tiled=True)  93.9 us
    all_to_all x3, blocking collectives, gather_rows(): got = lax.all_to_all(spread, axis_name, 0, 0, tiled=True)  93.3 us
    all_to_all x1, waiting for transfers between devices, on_device(): lax.all_to_all(back_flat.astype(jnp.bfloat16).reshape(col_count, 2 * bloc...  67.2 us
    all_to_all x1, waiting for transfers between devices, gather_rows(): got = lax.all_to_all(spread, axis_name, 0, 0, tiled=True)  41.8 us
    all_to_all x1, waiting for transfers between devices, on_device(): got = lax.all_to_all(payload, 'col', 0, 0, tiled=True)  33.5 us
    all_to_all x1, waiting for transfers between devices, scatter_sum(): got = lax.all_to_all(blocks, axis_name, 0, 0, tiled=True)  28.1 us
    all_to_all x1, starting transfers between devices, gather_rows(): got = lax.all_to_all(spread, axis_name, 0, 0, tiled=True)  11.4 us
  transfers between devices with their start and end apart: 8, of which 5 were waited for; matrix products, arithmetic and copies ran while one was open for 10% of the time, Pallas kernels for 0%

commit v1 on v0

--- a/solution.py
+++ b/solution.py
@@ -6,6 +6,22 @@
 EXPERTS = 4
 gelu_scale = 0.7978845608028654
 gelu_cubic = 0.044715
+
+
+def swapped_with_each(value, axis, split, join):
+    ways, here = (lax.axis_size(axis), lax.axis_index(axis))
+    width = value.shape[split] // ways
+    dims = list(value.shape)
+    dims[split] = width
+    height = dims[join]
+    dims[join] = height * ways
+    full = jnp.zeros(dims, value.dtype)
+    for mask in range(ways):
+        part = lax.dynamic_slice_in_dim(value, (here ^ mask) * width, width, axis=split)
+        if mask:
+            part = lax.ppermute(part, axis, [(d, d ^ mask) for d in range(ways)])
+        full = lax.dynamic_update_slice_in_dim(full, part, (here ^ mask) * height, axis=join)
+    return full
 
 
 def gelu_tanh(value):
@@ -62,7 +78,7 @@
     arrays, tok, width = pair.shape
     block = tok // count
     parts = pair.reshape(arrays, count, block, width).transpose(1, 0, 2, 3)
-    got = lax.all_to_all(parts.reshape(count, arrays * block, width), "row", 0, 0, tiled=True)
+    got = swapped_with_each(parts.reshape(count, arrays * block, width), "row", 0, 0)
     got = got.reshape(count, arrays, block, width).transpose(1, 2, 0, 3)
     return got.reshape(arrays, block, count * width)
 

time: 491 us -> 500 us (1.018)
  starting transfers between devices: 33 us -> 43.4 us
  blocking collectives: 196 us -> 190 us
    ppermute x0 -> x14, starting transfers between devices: none -> 14.5 us  [swapped_with_each(): part = lax.ppermute(part, axis, [(d, d ^ mask) for d in range(ways)])]
    all_to_all x1 -> x0, blocking collectives: 8.78 us -> none  [swap_blocks(): lax.all_to_all(parts.reshape(count, arrays * block, width), 'row', 0, 0,...]
    ppermute x0 -> x14, waiting for transfers between devices: none -> 8.11 us  [swapped_with_each(): part = lax.ppermute(part, axis, [(d, d ^ mask) for d in range(ways)])]
  transfers between devices with their start and end apart: 8 -> 21, of which waited for: 5 -> 7; matrix products, arithmetic and copies ran while one was open for 10% -> 10% of each run, Pallas kernels for 0% -> 0%
where the time goes in v1:
time: 500 us; the launch traced here: 499 us
  blocking collectives  190 us (38%)
  waiting for transfers between devices  178 us (36%)
  starting transfers between devices  43.4 us (9%)
  matrix products  35.1 us (7%)
  local copies, waits for them, and re-layouts  24.4 us (5%)
  between operations  14.4 us (3%)
  other arithmetic  13.4 us (3%)
    all_to_all x3, blocking collectives, scatter_sum(): got = lax.all_to_all(blocks, axis_name, 0, 0, tiled=True)  96.6 us
    all_to_all x3, blocking collectives, gather_rows(): got = lax.all_to_all(spread, axis_name, 0, 0, tiled=True)  93.3 us
    all_to_all x1, waiting for transfers between devices, on_device(): lax.all_to_all(back_flat.astype(jnp.bfloat16).reshape(col_count, 2 * bloc...  67 us
    all_to_all x1, waiting for transfers between devices, gather_rows(): got = lax.all_to_all(spread, axis_name, 0, 0, tiled=True)  40.7 us
    all_to_all x1, waiting for transfers between devices, on_device(): got = lax.all_to_all(payload, 'col', 0, 0, tiled=True)  33.7 us
    all_to_all x1, waiting for transfers between devices, scatter_sum(): got = lax.all_to_all(blocks, axis_name, 0, 0, tiled=True)  28.1 us
    ppermute x14, starting transfers between devices, swapped_with_each(): part = lax.ppermute(part, axis, [(d, d ^ mask) for d in range(ways)])  14.5 us
    all_to_all x1, starting transfers between devices, gather_rows(): got = lax.all_to_all(spread, axis_name, 0, 0, tiled=True)  11.4 us
  transfers between devices with their start and end apart: 21, of which 7 were waited for; matrix products, arithmetic and copies ran while one was open for 10% of the time, Pallas kernels for 0%

profile of v1, /device:TPU:32, one launch (start us, length us, event | category | flops | bytes accessed | tf_op | source)
XLA Modules:
  0.0 498.8 jit_solution(8852873961588842620)
XLA Ops:
  7.2 1.0 reshape_transpose_reshape_broadcast_in_dim.6
  8.3 2.3 collective-permute-start.6
  11.2 1.6 collective-permute-start.4
  12.8 1.7 collective-permute-start.3
  16.0 1.6 collective-permute-start.1
  18.3 1.4 collective-permute-done.1
  21.0 2.2 broadcast_in_dim.14
  23.2 11.4 %all-to-all-start = ((bf16[32,32,768]{2,1,0:T(8,128)(2,1)}), bf16[32,32,768]{2,1,0:T(8,128)(2,1)}, u32[]{:S(2)}, u32[]{:S(2)}) async-start(bf16[32,32,768]{2,1,0:T(8,128)(2,1)} %broadcast_in_dim.14), calls=%async_computation | async-start | bytes 3145728 | tf_op jit(solution)/shard_map/all_to_all | solution.py:49
  35.4 40.7 %all-to-all-done = bf16[32,32,768]{2,1,0:T(8,128)(2,1)} async-done(((bf16[32,32,768]{2,1,0:T(8,128)(2,1)}), bf16[32,32,768]{2,1,0:T(8,128)(2,1)}, u32[]{:S(2)}, u32[]{:S(2)}) %all-to-all-start) | async-done | bytes 1572896 | tf_op jit(solution)/shard_map/all_to_all | solution.py:49
  76.1 3.1 convolution_convert_fusion.2
  79.2 26.5 %all_to_all.50 = bf16[8,128,768]{2,1,0:T(8,128)(2,1)S(1)} all-to-all(bf16[8,128,768]{2,1,0:T(8,128)(2,1)S(1)} %bitcast.112), channel_id=1, replica_groups=mesh['row'=8,'col'=32] {'row'}, dimensions={0} | all-to-all | bytes 3145728 | tf_op jit(solution)/shard_map/all_to_all | solution.py:56
  106.2 24.2 %all_to_all.51 = bf16[8,128,768]{2,1,0:T(8,128)(2,1)S(1)} all-to-all(bf16[8,128,768]{2,1,0:T(8,128)(2,1)S(1)} %broadcast_in_dim.15), channel_id=1, replica_groups=mesh['row'=8,'col'=32] {'row'}, dimensions={0} | all-to-all | bytes 3145728 | tf_op jit(solution)/shard_map/all_to_all | solution.py:49
  130.3 1.2 copy-done.4
  131.5 2.6 fusion.38
  134.1 45.7 %all_to_all.52 = bf16[32,32,768]{2,1,0:T(8,128)(2,1)S(1)} all-to-all(bf16[32,32,768]{2,1,0:T(8,128)(2,1)} %bitcast.111), channel_id=1, replica_groups=mesh['row'=8,'col'=32] {'col'}, dimensions={0} | all-to-all | bytes 3145728 | tf_op jit(solution)/shard_map/all_to_all | solution.py:56
  181.3 1.4 reshape_transpose_reshape_broadcast_in_dim.7
  184.3 1.3 collective-permute-start.13
  185.6 2.1 collective-permute-start.12
  187.7 2.9 collective-permute-start.10
  190.6 3.6 collective-permute-done.8
  194.2 3.0 collective-permute-done.9
  197.4 1.9 broadcast_in_dim.18
  199.3 4.9 all-to-all-start.4
  205.8 3.7 slice.17
  209.6 33.7 %all-to-all-done.4 = bf16[32,4,6144]{2,1,0:T(4,128)(2,1)} async-done(((bf16[32,4,6144]{2,1,0:T(4,128)(2,1)}), bf16[32,4,6144]{2,1,0:T(4,128)(2,1)}, u32[]{:S(2)}, u32[]{:S(2)}) %all-to-all-start.4) | async-done | bytes 1572896 | tf_op jit(solution)/shard_map/all_to_all | solution.py:140
  243.3 3.4 multiply_convert_fusion.8
  247.3 4.1 fusion.4
  251.5 0.9 copy.128
  252.4 4.0 fusion.15
  257.0 1.0 fusion.31
  258.0 1.1 fusion
  259.1 1.9 copy.120
  260.9 7.2 %all-to-all-start.5 = ((bf16[256,8,768]{2,1,0:T(8,128)(2,1)}), bf16[256,8,768]{2,1,0:T(8,128)(2,1)S(1)}, u32[]{:S(2)}, u32[]{:S(2)}) async-start(bf16[256,8,768]{2,1,0:T(8,128)(2,1)} %bitcast.33), calls=%async_computation.5 | async-start | bytes 6291456 | tf_op jit(solution)/shard_map/all_to_all | solution.py:171
  268.4 5.4 %fusion.2 = f32[6144,256]{1,0:T(8,128)} fusion(bf16[32,4,256]{2,0,1:T(8,128)(2,1)} %copy-done.16, bf16[32,4,6144]{2,1,0:T(4,128)(2,1)} %all-to-all-done.4), kind=kOutput, calls=%fused_computation.5 | convolution fusion | flops 405798912 | bytes 7929856 | tf_op jit(solution)/shard_map/dot_general | solution.py:160
  276.5 67.0 %all-to-all-done.5 = bf16[256,8,768]{2,1,0:T(8,128)(2,1)S(1)} async-done(((bf16[256,8,768]{2,1,0:T(8,128)(2,1)}), bf16[256,8,768]{2,1,0:T(8,128)(2,1)S(1)}, u32[]{:S(2)}, u32[]{:S(2)}) %all-to-all-start.5) | async-done | bytes 3145760 | tf_op jit(solution)/shard_map/all_to_all | solution.py:171
  344.4 2.3 slice_reduce_fusion
  347.6 44.9 %all_to_all.53 = bf16[32,32,768]{2,1,0:T(8,128)(2,1)S(1)} all-to-all(bf16[32,32,768]{2,1,0:T(8,128)(2,1)S(1)} %broadcast_in_dim.19), channel_id=1, replica_groups=mesh['row'=8,'col'=32] {'col'}, dimensions={0} | all-to-all | bytes 3145728 | tf_op jit(solution)/shard_map/all_to_all | solution.py:49
  392.5 1.4 convolution_convert_fusion.1
  394.0 24.4 %all_to_all.54 = bf16[8,128,768]{2,1,0:T(8,128)(2,1)S(1)} all-to-all(bf16[8,128,768]{2,1,0:T(8,128)(2,1)S(1)} %bitcast.113), channel_id=1, replica_groups=mesh['row'=8,'col'=32] {'row'}, dimensions={0} | all-to-all | bytes 3145728 | tf_op jit(solution)/shard_map/all_to_all | solution.py:56
  419.0 24.2 %all_to_all.55 = bf16[8,128,768]{2,1,0:T(8,128)(2,1)S(1)} all-to-all(bf16[8,128,768]{2,1,0:T(8,128)(2,1)S(1)} %broadcast_in_dim.20), channel_id=1, replica_groups=mesh['row'=8,'col'=32] {'row'}, dimensions={0} | all-to-all | bytes 3145728 | tf_op jit(solution)/shard_map/all_to_all | solution.py:49
  443.1 2.6 convolution_convert_fusion
  445.8 5.1 %all-to-all-start.9 = ((bf16[32,32,768]{2,1,0:T(8,128)(2,1)}), bf16[32,32,768]{2,1,0:T(8,128)(2,1)}, u32[]{:S(2)}, u32[]{:S(2)}) async-start(bf16[32,32,768]{2,1,0:T(8,128)(2,1)} %bitcast.39), calls=%async_computation.9 | async-start | bytes 3145728 | tf_op jit(solution)/shard_map/all_to_all | solution.py:56
  451.6 2.5 convolution_convert_fusion.3
  454.0 3.9 convolution_convert_fusion.4
  457.9 2.1 convert_element_type.172
  460.0 1.9 convert_element_type.169
  461.9 28.1 %all-to-all-done.9 = bf16[32,32,768]{2,1,0:T(8,128)(2,1)} async-done(((bf16[32,32,768]{2,1,0:T(8,128)(2,1)}), bf16[32,32,768]{2,1,0:T(8,128)(2,1)}, u32[]{:S(2)}, u32[]{:S(2)}) %all-to-all-start.9) | async-done | bytes 1572896 | tf_op jit(solution)/shard_map/all_to_all | solution.py:56
  490.0 1.6 convert_reduce_fusion
  (131 shorter events, 17.8 us)
Async XLA Ops:
  7.2 236.1 %copy-start = (bf16[6144,256]{1,0:T(8,128)(2,1)S(1)}, bf16[6144,256]{1,0:T(8,128)(2,1)}, u32[]{:S(2)}) copy-start(bf16[6144,256]{1,0:T(8,128)(2,1)} %param.11) | copy-start | bytes 9437188
  8.3 7.8 %collective-permute-start.6 = (bf16[1,4,768]{2,1,0:T(4,128)(2,1)S(1)}, bf16[1,4,768]{2,1,0:T(4,128)(2,1)S(1)}, u32[]{:S(2)}, u32[]{:S(2)}) collective-permute-start(bf16[1,4,768]{2,1,0:T(4,128)(2,1)S(1)} %get-tuple-element.21), channel_id=1, source_target_pairs={{0,224},{32,192},{64,160},{96,128},{128,96},{160,64},{192,32},{224... | collective-permute-start | bytes 18440 | tf_op jit(solution)/shard_map/ppermute | solution.py:22
  10.6 7.1 %collective-permute-start.5 = (bf16[1,4,768]{2,1,0:T(4,128)(2,1)S(1)}, bf16[1,4,768]{2,1,0:T(4,128)(2,1)S(1)}, u32[]{:S(2)}, u32[]{:S(2)}) collective-permute-start(bf16[1,4,768]{2,1,0:T(4,128)(2,1)S(1)} %get-tuple-element.22), channel_id=1, source_target_pairs={{0,192},{32,224},{64,128},{96,160},{128,64},{160,96},{192,0},{224,... | collective-permute-start | bytes 18440 | tf_op jit(solution)/shard_map/ppermute | solution.py:22
  11.2 7.0 %collective-permute-start.4 = (bf16[1,4,768]{2,1,0:T(4,128)(2,1)S(1)}, bf16[1,4,768]{2,1,0:T(4,128)(2,1)S(1)}, u32[]{:S(2)}, u32[]{:S(2)}) collective-permute-start(bf16[1,4,768]{2,1,0:T(4,128)(2,1)S(1)} %get-tuple-element.23), channel_id=1, source_target_pairs={{0,160},{32,128},{64,224},{96,192},{128,32},{160,0},{192,96},{224,... | collective-permute-start | bytes 18440 | tf_op jit(solution)/shard_map/ppermute | solution.py:22
  12.8 5.4 %collective-permute-start.3 = (bf16[1,4,768]{2,1,0:T(4,128)(2,1)S(1)}, bf16[1,4,768]{2,1,0:T(4,128)(2,1)S(1)}, u32[]{:S(2)}, u32[]{:S(2)}) collective-permute-start(bf16[1,4,768]{2,1,0:T(4,128)(2,1)S(1)} %get-tuple-element.24), channel_id=1, source_target_pairs={{0,128},{32,160},{64,192},{96,224},{128,0},{160,32},{192,64},{224,... | collective-permute-start | bytes 18440 | tf_op jit(solution)/shard_map/ppermute | solution.py:22
  14.6 3.7 collective-permute-start.2
  16.0 3.6 collective-permute-start.1
  17.7 2.0 collective-permute-start
  23.2 52.9 %all-to-all-start = ((bf16[32,32,768]{2,1,0:T(8,128)(2,1)}), bf16[32,32,768]{2,1,0:T(8,128)(2,1)}, u32[]{:S(2)}, u32[]{:S(2)}) async-start(bf16[32,32,768]{2,1,0:T(8,128)(2,1)} %broadcast_in_dim.14), calls=%async_computation | async-start | bytes 3145728 | tf_op jit(solution)/shard_map/all_to_all | solution.py:49
  34.6 99.5 %all-gather.4.cloned.1.call-start = ((), (), s32[]{:S(2)}) async-start(), calls=%async_computation.14 | async-start | bytes 3244032 | tf_op jit(solution)/shard_map/all_gather | solution.py:120
  106.2 25.4 %copy-start.20 = (bf16[768,768]{1,0:T(8,128)(2,1)S(1)}, bf16[768,768]{1,0:T(8,128)(2,1)}, u32[]{:S(2)}) copy-start(bf16[768,768]{1,0:T(8,128)(2,1)} %param.10) | copy-start | bytes 3538948
  130.3 1.2 copy-start.4
  179.8 0.8 copy-start.14
  183.5 7.0 %collective-permute-start.7 = (bf16[1,4,768]{2,1,0:T(4,128)(2,1)S(1)}, bf16[1,4,768]{2,1,0:T(4,128)(2,1)S(1)}, u32[]{:S(2)}, u32[]{:S(2)}) collective-permute-start(bf16[1,4,768]{2,1,0:T(4,128)(2,1)S(1)} %get-tuple-element.20), channel_id=1, source_target_pairs={{0,32},{32,0},{64,96},{96,64},{128,160},{160,128},{192,224},{224,1... | collective-permute-start | bytes 18440 | tf_op jit(solution)/shard_map/ppermute | solution.py:22
  184.3 13.0 %collective-permute-start.13 = (bf16[1,4,768]{2,1,0:T(4,128)(2,1)S(1)}, bf16[1,4,768]{2,1,0:T(4,128)(2,1)S(1)}, u32[]{:S(2)}, u32[]{:S(2)}) collective-permute-start(bf16[1,4,768]{2,1,0:T(4,128)(2,1)S(1)} %get-tuple-element.14), channel_id=1, source_target_pairs={{0,224},{32,192},{64,160},{96,128},{128,96},{160,64},{192,32},{224... | collective-permute-start | bytes 18440 | tf_op jit(solution)/shard_map/ppermute | solution.py:22
  185.6 11.7 %collective-permute-start.12 = (bf16[1,4,768]{2,1,0:T(4,128)(2,1)S(1)}, bf16[1,4,768]{2,1,0:T(4,128)(2,1)S(1)}, u32[]{:S(2)}, u32[]{:S(2)}) collective-permute-start(bf16[1,4,768]{2,1,0:T(4,128)(2,1)S(1)} %get-tuple-element.15), channel_id=1, source_target_pairs={{0,192},{32,224},{64,128},{96,160},{128,64},{160,96},{192,0},{224,... | collective-permute-start | bytes 18440 | tf_op jit(solution)/shard_map/ppermute | solution.py:22
  187.7 9.6 %collective-permute-start.11 = (bf16[1,4,768]{2,1,0:T(4,128)(2,1)S(1)}, bf16[1,4,768]{2,1,0:T(4,128)(2,1)S(1)}, u32[]{:S(2)}, u32[]{:S(2)}) collective-permute-start(bf16[1,4,768]{2,1,0:T(4,128)(2,1)S(1)} %get-tuple-element.16), channel_id=1, source_target_pairs={{0,160},{32,128},{64,224},{96,192},{128,32},{160,0},{192,96},{224,... | collective-permute-start | bytes 18440 | tf_op jit(solution)/shard_map/ppermute | solution.py:22
  187.7 9.6 %collective-permute-start.10 = (bf16[1,4,768]{2,1,0:T(4,128)(2,1)S(1)}, bf16[1,4,768]{2,1,0:T(4,128)(2,1)S(1)}, u32[]{:S(2)}, u32[]{:S(2)}) collective-permute-start(bf16[1,4,768]{2,1,0:T(4,128)(2,1)S(1)} %get-tuple-element.17), channel_id=1, source_target_pairs={{0,128},{32,160},{64,192},{96,224},{128,0},{160,32},{192,64},{224,... | collective-permute-start | bytes 18440 | tf_op jit(solution)/shard_map/ppermute | solution.py:22
  190.5 3.6 collective-permute-start.8
  194.2 3.1 collective-permute-start.9
  199.3 44.0 %all-to-all-start.4 = ((bf16[32,4,6144]{2,1,0:T(4,128)(2,1)}), bf16[32,4,6144]{2,1,0:T(4,128)(2,1)}, u32[]{:S(2)}, u32[]{:S(2)}) async-start(bf16[32,4,6144]{2,1,0:T(4,128)(2,1)} %broadcast_in_dim.18), calls=%async_computation.4 | async-start | bytes 3145728 | tf_op jit(solution)/shard_map/all_to_all | solution.py:140
  204.2 253.8 %reduce-scatter.5.cloned.1.call-start = ((), (), s32[]{:S(2)}) async-start(), calls=%async_computation.13 | async-start | bytes 7077888 | tf_op jit(solution)/shard_map/reduce_scatter | solution.py:199
  205.8 3.7 copy-start.17
  243.3 4.1 copy-start.2
  246.7 0.6 copy-start.13
  252.4 4.6 copy-start.3
  256.4 0.6 copy-start.16
  260.9 82.6 %all-to-all-start.5 = ((bf16[256,8,768]{2,1,0:T(8,128)(2,1)}), bf16[256,8,768]{2,1,0:T(8,128)(2,1)S(1)}, u32[]{:S(2)}, u32[]{:S(2)}) async-start(bf16[256,8,768]{2,1,0:T(8,128)(2,1)} %bitcast.33), calls=%async_computation.5 | async-start | bytes 6291456 | tf_op jit(solution)/shard_map/all_to_all | solution.py:171
  268.1 191.9 %reduce-scatter.3.cloned.1.call-start = ((), (), s32[]{:S(2)}) async-start(), calls=%async_computation.12 | async-start | bytes 7077888 | tf_op jit(solution)/shard_map/reduce_scatter | solution.py:196
  273.8 0.7 copy-start.19
  273.8 0.7 copy-start.18
  343.5 0.9 copy-start.8
  344.4 2.3 copy-start.15
  346.8 0.6 copy-start.9
  347.6 45.0 %copy-start.21 = (bf16[768,768]{1,0:T(8,128)(2,1)S(1)}, bf16[768,768]{1,0:T(8,128)(2,1)}, u32[]{:S(2)}) copy-start(bf16[768,768]{1,0:T(8,128)(2,1)} %param.10) | copy-start | bytes 3538948
  419.0 24.2 %copy-start.22 = (bf16[768,768]{1,0:T(8,128)(2,1)S(1)}, bf16[768,768]{1,0:T(8,128)(2,1)}, u32[]{:S(2)}) copy-start(bf16[768,768]{1,0:T(8,128)(2,1)} %param.9) | copy-start | bytes 3538948
  443.1 2.6 copy-start.6
  445.8 5.1 %copy-start.12 = (f32[8,4,768]{2,1,0:T(4,128)S(1)}, f32[8,4,768]{2,1,0:T(4,128)}, u32[]{:S(2)}) copy-start(f32[8,4,768]{2,1,0:T(4,128)} %get-tuple-element.13) | copy-start | bytes 294916
  445.8 5.2 %copy-start.11 = (bf16[32,768]{1,0:T(8,128)(2,1)S(1)}, bf16[32,768]{1,0:T(8,128)(2,1)}, u32[]{:S(2)}) copy-start(bf16[32,768]{1,0:T(8,128)(2,1)} %add_convert_fusion.3) | copy-start | bytes 147460
  445.8 5.8 %copy-start.5 = (bf16[8,128,768]{2,1,0:T(8,128)(2,1)S(1)}, bf16[8,128,768]{2,1,0:T(8,128)(2,1)}, u32[]{:S(2)}) copy-start(bf16[8,128,768]{2,1,0:T(8,128)(2,1)} %copy-done.4) | copy-start | bytes 4718596
  445.8 44.2 %all-to-all-start.9 = ((bf16[32,32,768]{2,1,0:T(8,128)(2,1)}), bf16[32,32,768]{2,1,0:T(8,128)(2,1)}, u32[]{:S(2)}, u32[]{:S(2)}) async-start(bf16[32,32,768]{2,1,0:T(8,128)(2,1)} %bitcast.39), calls=%async_computation.9 | async-start | bytes 3145728 | tf_op jit(solution)/shard_map/all_to_all | solution.py:56
  451.6 2.5 copy-start.7
  457.9 34.4 %copy-start.1 = (bf16[6144,256]{1,0:T(8,128)(2,1)S(1)}, bf16[6144,256]{1,0:T(8,128)(2,1)}, u32[]{:S(2)}) copy-start(bf16[6144,256]{1,0:T(8,128)(2,1)} %param.11) | copy-start | bytes 9437188
  460.0 31.7 %copy-start.10 = (bf16[32,768]{1,0:T(8,128)(2,1)S(1)}, bf16[32,768]{1,0:T(8,128)(2,1)}, u32[]{:S(2)}) copy-start(bf16[32,768]{1,0:T(8,128)(2,1)} %copy-done.9) | copy-start | bytes 147460
Sparse Core Ops, SparseCore 0:
  38.6 82.3 all-gather.3
  251.6 62.6 reduce-scatter.4
  316.9 50.1 reduce-scatter.2
